TPU v7x, 512 devices: a whole 4x4x16 slice. The times are simulated.
512 devices in a mesh: dp: 64 (over z, x), pair: 8 (over y, core).
Axes of the slice: x: 4, y: 4, z: 16, core: 2. Of those that a mesh axis runs over, the one named last changes fastest.
Arguments:
- embedding: bfloat16 [65536, 1024], P(('dp', 'pair')), may hold values from -32 to 32
- labels: int32 [65536], P(('dp', 'pair')), may hold values from 0 to 127, as said below
- order_ids: int32 [65536], P(('dp', 'pair')), may hold values from 0 to 65535, each once
Outputs:
- best_similarity: float32 [65536], P(('dp', 'pair'))
Inputs may be any that keep to these rules, and one draw needn't show every extreme that they name: `labels`: clusters 2 * g to 2 * g + 1 form owner group g. Among the 128 rows of one device (aligned blocks of the whole array) at most 4 name clusters of any one group, and in every draw some group gets exactly 4 rows from every device.
All inputs are finite; a program needn't handle non-finite values.
Results may differ from a plain program's by a relative error of at most 0.00049.
Values may be sent and summed in bfloat16 or wider, within the bound.
No kernel may reach another device: no remote copies, remote signals or barrier semaphores. Data moves between devices by JAX's collectives and lax.ppermute only.
A program may use at most 64 MiB of HBM per device.

v0:
```python
import jax
import jax.numpy as jnp
from jax import lax
from jax.sharding import PartitionSpec as P

CL_OWN = 2
META = 128
PUBLISH_ROWS = 32


def tile_best(own_rows, own_key, other_rows, other_key, rows_total):
    scores = jnp.dot(own_rows, other_rows.T, preferred_element_type=jnp.float32)
    same_cluster = other_key[None, :] // rows_total == own_key[:, None] // rows_total
    earlier = same_cluster & (other_key[None, :] < own_key[:, None])
    return jnp.max(jnp.where(earlier, scores, -1.0), axis=1)


def slot_keys(rows, width, rows_total):
    meta = rows[:, width : width + 3].astype(jnp.int32)
    return meta[:, 0] * rows_total + meta[:, 1] * 256 + meta[:, 2]


def on_device(embedding, labels, order_ids):
    groups = lax.axis_size("dp")
    pairs = lax.axis_size("pair")
    rows_here, width = embedding.shape
    rows_total = rows_here * groups * pairs
    capacity = 2 * rows_here // groups
    slot_count = groups * capacity
    values = embedding.astype(jnp.float32)
    squares = jnp.sum(values * values, axis=1, keepdims=True)
    shifted = squares + 1e-06
    unit_rows = (values * lax.rsqrt(shifted)).astype(jnp.bfloat16)
    owner_group = labels // CL_OWN
    onehot = (owner_group[:, None] == jnp.arange(groups, dtype=jnp.int32)[None, :]).astype(
        jnp.int32
    )
    before = jnp.cumsum(onehot, axis=0) - onehot
    slot_index = owner_group * capacity + jnp.sum(before * onehot, axis=1)
    meta = jnp.stack([labels + 1, order_ids // 256, order_ids % 256], axis=1).astype(jnp.bfloat16)
    meta = jnp.pad(meta, ((0, 0), (0, META - 3)))
    packed = jnp.concatenate([unit_rows, meta], axis=1)
    send_rows = jnp.zeros((slot_count, width + META), jnp.bfloat16).at[slot_index].set(packed)
    got_rows = lax.all_to_all(
        send_rows.reshape(groups, capacity, -1), "dp", split_axis=0, concat_axis=0, tiled=True
    ).reshape(slot_count, -1)
    piece_rows = lax.all_gather(got_rows, "pair", axis=0, tiled=True)
    got_key = slot_keys(got_rows, width, rows_total)
    piece_key = slot_keys(piece_rows, width, rows_total)
    column = lax.broadcasted_iota(jnp.int32, got_rows.shape, 1)
    query_rows = jnp.where(column < width, got_rows, jnp.zeros_like(got_rows))
    best_seen = jnp.full((slot_count,), -1.0, jnp.float32)
    piece_count = piece_rows.shape[0]
    for offset in range(0, piece_count, 512):
        width_now = min(512, piece_count - offset)
        found = tile_best(
            query_rows,
            got_key,
            piece_rows[offset : offset + width_now],
            piece_key[offset : offset + width_now],
            rows_total,
        )
        best_seen = jnp.maximum(best_seen, found)
    publish = jnp.zeros((PUBLISH_ROWS * 128,), jnp.float32).at[:slot_count].set(best_seen)
    published = lax.all_gather(publish.reshape(PUBLISH_ROWS, 128), "dp", axis=0, tiled=False)
    me = lax.axis_index("dp")
    answered = lax.dynamic_slice_in_dim(
        published.reshape(groups, PUBLISH_ROWS * 128), me * capacity, capacity, axis=1
    )
    return answered.reshape(slot_count)[slot_index]


def solution(mesh):
    in_specs = (P(("dp", "pair"), None), P(("dp", "pair")), P(("dp", "pair")))
    out_specs = P(("dp", "pair"))
    return jax.shard_map(
        on_device, mesh=mesh, in_specs=in_specs, out_specs=out_specs, check_vma=False
    )
```

profile of v0, /device:TPU:8, one launch (start us, length us, event | category | flops | bytes accessed | tf_op | source)
XLA Modules:
  0.0 256.4 jit_solution(14375752796550664068)
XLA Ops:
  6.5 0.0 all-gather.3.cloned.1.call-start
  6.5 0.7 convert_bitcast_fusion.1
  7.2 0.1 fusion.36
  7.3 0.2 reduce_window_sum.11
  7.5 0.2 select_reduce_fusion
  7.7 0.7 convert_bitcast_fusion
  8.3 0.1 copy.7
  8.5 1.1 fusion.18
  9.6 1.1 fusion.19
  10.6 1.3 scatter_custom_fusion
  12.0 0.1 reshape.149
  12.1 54.0 %all_to_all.5 = bf16[64,4,1152]{2,1,0:T(4,128)(2,1)S(1)} all-to-all(bf16[64,4,1152]{2,1,0:T(4,128)(2,1)S(1)} %reshape.149), channel_id=1, replica_groups=mesh['dp'=64,'pair'=8] {'dp'}, dimensions={0} | all-to-all | bytes 1179648 | tf_op jit(solution)/shard_map/all_to_all | solution.py:44
  66.1 1.0 reshape.150
  67.1 0.0 copy-start
  67.1 0.0 all-gather.3.cloned.1.call-update
  67.1 0.0 all-gather.5.cloned.1.call-start
  67.2 0.9 slice_convert_fusion.1
  68.1 0.3 fusion.33
  68.4 31.6 %all-gather.3.cloned.1.call-done = bf16[2048,1152]{1,0:T(8,128)(2,1)} async-done(((bf16[256,1152]{1,0:T(8,128)(2,1)}), bf16[2048,1152]{1,0:T(8,128)(2,1)}) %all-gather.3.cloned.1.call-update) | async-done | bytes 4718608 | tf_op jit(solution)/shard_map/all_gather | solution.py:47
  99.9 0.0 copy-start.1
  99.9 1.3 slice_convert_fusion
  101.2 0.6 slice_add_fusion
  101.8 0.4 slice_reduce_fusion.3
  102.2 0.0 copy-done
  102.2 0.2 copy-done.1
  102.4 0.6 fusion.4
  103.1 0.6 fusion.7
  103.7 0.6 fusion.10
  104.4 0.6 fusion.13
  105.0 0.6 pad_bitcast_fusion
  105.6 0.0 all-gather.5.cloned.1.call-update
  105.7 140.1 %all-gather.5.cloned.1.call-done = f32[64,32,128]{2,1,0:T(8,128)} async-done(((f32[1,32,128]{2,1,0:T(8,128)}), f32[64,32,128]{2,1,0:T(8,128)}) %all-gather.5.cloned.1.call-update) | async-done | bytes 1048592 | tf_op jit(solution)/shard_map/all_gather | solution.py:65
  245.8 1.8 copy.10
  247.6 0.1 constant_dynamic-slice_fusion
  247.7 0.1 reshape.152
  247.8 1.8 gather_fusion
  (8 shorter events, 0.1 us)
Async XLA Ops:
  6.5 93.4 %all-gather.3.cloned.1.call-start = ((), (), s32[]{:S(2)}) async-start(), calls=%async_computation.1 | async-start | bytes 5308416 | tf_op jit(solution)/shard_map/all_gather | solution.py:47
  67.1 35.1 %copy-start = (bf16[256,1152]{1,0:T(8,128)(2,1)S(1)}, bf16[256,1152]{1,0:T(8,128)(2,1)}, u32[]{:S(2)}) copy-start(bf16[256,1152]{1,0:T(8,128)(2,1)} %reshape.150) | copy-start | bytes 1769476
  67.1 178.7 %all-gather.5.cloned.1.call-start = ((), (), s32[]{:S(2)}) async-start(), calls=%async_computation.2 | async-start | bytes 1064960 | tf_op jit(solution)/shard_map/all_gather | solution.py:65
  99.9 2.5 copy-start.1
Sparse Core Ops, SparseCore 0:
  67.2 32.6 all-gather.2
  105.8 139.9 all-gather.4
where the time goes:
time: 257 us; the launch traced here: 256 us
  waiting for transfers between devices  172 us (67%)
  blocking collectives  54 us (21%)
  between operations  13.5 us (5%)
  other arithmetic  8.4 us (3%)
  local copies, waits for them, and re-layouts  6.2 us (2%)
    all_gather x1, waiting for transfers between devices, on_device(): lax.all_gather(publish.reshape(PUBLISH_ROWS, 128), 'dp', axis=0, tiled=Fa...  140 us
    all_to_all x1, blocking collectives, on_device(): lax.all_to_all(send_rows.reshape(groups, capacity, -1), 'dp', split_axis=...  54 us
    all_gather x1, waiting for transfers between devices, on_device(): piece_rows = lax.all_gather(got_rows, 'pair', axis=0, tiled=True)  31.6 us
  transfers between devices with their start and end apart: 2, of which 2 were waited for; matrix products, arithmetic and copies ran while one was open for 0% of the time, Pallas kernels for 0%

commit v1 on v0

--- a/solution.py
+++ b/solution.py
@@ -6,6 +6,13 @@
 CL_OWN = 2
 META = 128
 PUBLISH_ROWS = 32
+
+
+def exchange_gather(shard, mesh_axis, dim):
+    peers = lax.axis_size(mesh_axis)
+    blocks = jnp.stack([shard for _ in range(peers)])
+    blocks = lax.all_to_all(blocks, mesh_axis, split_axis=0, concat_axis=0)
+    return jnp.concatenate(blocks, axis=dim)
 
 
 def tile_best(own_rows, own_key, other_rows, other_key, rows_total):
@@ -44,7 +51,7 @@
     got_rows = lax.all_to_all(
         send_rows.reshape(groups, capacity, -1), "dp", split_axis=0, concat_axis=0, tiled=True
     ).reshape(slot_count, -1)
-    piece_rows = lax.all_gather(got_rows, "pair", axis=0, tiled=True)
+    piece_rows = exchange_gather(got_rows, "pair", 0)
     got_key = slot_keys(got_rows, width, rows_total)
     piece_key = slot_keys(piece_rows, width, rows_total)
     column = lax.broadcasted_iota(jnp.int32, got_rows.shape, 1)

time: 257 us -> 284 us (1.11)
  local copies, waits for them, and re-layouts: 6.2 us -> 17.5 us
  waiting for transfers between devices: 172 us -> 183 us
  starting transfers between devices: 0.04 us -> 4.92 us
    all_to_all x0 -> x1, waiting for transfers between devices: none -> 53.3 us  [exchange_gather(): blocks = lax.all_to_all(blocks, mesh_axis, split_axis=0, concat_axis=0)]
    all_gather x1 -> x0, waiting for transfers between devices: 31.6 us -> none  [on_device(): piece_rows = lax.all_gather(got_rows, 'pair', axis=0, tiled=True)]
    all_gather x1, waiting for transfers between devices: 140 us -> 130 us  [on_device(): lax.all_gather(publish.reshape(PUBLISH_ROWS, 128), 'dp', axis=0, tiled=Fa...]
    all_to_all x0 -> x1, local copies, waits for them, and re-layouts: none -> 6.78 us  [exchange_gather(): blocks = lax.all_to_all(blocks, mesh_axis, split_axis=0, concat_axis=0)]
    all_to_all x0 -> x1, starting transfers between devices: none -> 4.92 us  [exchange_gather(): blocks = lax.all_to_all(blocks, mesh_axis, split_axis=0, concat_axis=0)]
    another operation x0 -> x3, local copies, waits for them, and re-layouts: none -> 2.85 us  [exchange_gather(): blocks = jnp.stack([shard for _ in range(peers)])]
where the time goes in v1:
time: 284 us; the launch traced here: 283 us
  waiting for transfers between devices  183 us (64%)
  blocking collectives  54 us (19%)
  local copies, waits for them, and re-layouts  17.5 us (6%)
  between operations  13.5 us (5%)
  other arithmetic  7.61 us (3%)
  starting transfers between devices  4.92 us (2%)
    all_gather x1, waiting for transfers between devices, on_device(): lax.all_gather(publish.reshape(PUBLISH_ROWS, 128), 'dp', axis=0, tiled=Fa...  130 us
    all_to_all x1, blocking collectives, on_device(): lax.all_to_all(send_rows.reshape(groups, capacity, -1), 'dp', split_axis=...  54 us
    all_to_all x1, waiting for transfers between devices, exchange_gather(): blocks = lax.all_to_all(blocks, mesh_axis, split_axis=0, concat_axis=0)  53.3 us
    all_to_all x1, local copies, waits for them, and re-layouts, exchange_gather(): blocks = lax.all_to_all(blocks, mesh_axis, split_axis=0, concat_axis=0)  6.78 us
  transfers between devices with their start and end apart: 2, of which 2 were waited for; matrix products, arithmetic and copies ran while one was open for 0% of the time, Pallas kernels for 0%

profile of v1, /device:TPU:8, one launch (start us, length us, event | category | flops | bytes accessed | tf_op | source)
XLA Modules:
  0.0 283.1 jit_solution(12305552172805881841)
XLA Ops:
  6.5 1.1 fusion.6
  7.6 0.7 convert_bitcast_fusion.1
  8.3 0.7 convert_bitcast_fusion
  9.0 0.1 copy.18
  9.1 0.1 fusion.20
  9.2 0.2 reduce_window_sum.11
  9.4 0.2 select_reduce_fusion
  9.6 1.1 fusion.7
  10.6 1.3 scatter_custom_fusion
  12.0 0.1 reshape.176
  12.1 54.0 %all_to_all.10 = bf16[64,4,1152]{2,1,0:T(4,128)(2,1)S(1)} all-to-all(bf16[64,4,1152]{2,1,0:T(4,128)(2,1)S(1)} %reshape.176), channel_id=1, replica_groups=mesh['dp'=64,'pair'=8] {'dp'}, dimensions={0} | all-to-all | bytes 1179648 | tf_op jit(solution)/shard_map/all_to_all | solution.py:51
  66.1 0.1 stack_reshape.2
  66.3 0.2 copy.12
  66.5 2.5 stack.23
  69.0 4.9 %all-to-all-start.1 = ((bf16[8,256,1152]{1,2,0:T(8,128)(2,1)}), bf16[8,256,1152]{1,2,0:T(8,128)(2,1)}, u32[]{:S(2)}, u32[]{:S(2)}) async-start(bf16[8,256,1152]{1,2,0:T(8,128)(2,1)} %stack.23), calls=%async_computation.1 | async-start | bytes 9437184 | tf_op jit(solution)/shard_map/all_to_all | solution.py:14
  73.9 0.0 all-gather.2.cloned.1.call-start
  73.9 0.2 broadcast_select_fusion
  74.2 0.1 select_n.80
  74.3 0.3 fusion.17
  74.6 53.3 %all-to-all-done.1 = bf16[8,256,1152]{1,2,0:T(8,128)(2,1)} async-done(((bf16[8,256,1152]{1,2,0:T(8,128)(2,1)}), bf16[8,256,1152]{1,2,0:T(8,128)(2,1)}, u32[]{:S(2)}, u32[]{:S(2)}) %all-to-all-start.1) | async-done | bytes 4718624 | tf_op jit(solution)/shard_map/all_to_all | solution.py:14
  127.9 6.8 %copy.13 = bf16[8,256,1152]{2,1,0:T(8,128)(2,1)} copy(bf16[8,256,1152]{1,2,0:T(8,128)(2,1)} %all-to-all-done.1) | data formatting | bytes 9437184 | tf_op jit(solution)/shard_map/all_to_all | solution.py:14
  134.7 2.7 fusion.32
  137.4 1.1 slice_convert_fusion
  138.5 0.6 slice_add_fusion
  139.1 0.4 slice_reduce_fusion.3
  139.5 0.6 fusion.1
  140.2 0.6 fusion.2
  140.8 0.6 fusion
  141.5 0.6 fusion.3
  142.1 0.6 pad_bitcast_fusion
  142.7 0.0 all-gather.2.cloned.1.call-update
  142.8 129.7 %all-gather.2.cloned.1.call-done = f32[64,32,128]{2,1,0:T(8,128)} async-done(((f32[1,32,128]{2,1,0:T(8,128)}), f32[64,32,128]{2,1,0:T(8,128)}) %all-gather.2.cloned.1.call-update) | async-done | bytes 1048592 | tf_op jit(solution)/shard_map/all_gather | solution.py:72
  272.5 1.8 copy.21
  274.3 0.1 constant_dynamic-slice_fusion
  274.4 0.1 reshape.179
  274.5 1.8 gather_fusion
  (9 shorter events, 0.1 us)
Async XLA Ops:
  69.0 58.9 %all-to-all-start.1 = ((bf16[8,256,1152]{1,2,0:T(8,128)(2,1)}), bf16[8,256,1152]{1,2,0:T(8,128)(2,1)}, u32[]{:S(2)}, u32[]{:S(2)}) async-start(bf16[8,256,1152]{1,2,0:T(8,128)(2,1)} %stack.23), calls=%async_computation.1 | async-start | bytes 9437184 | tf_op jit(solution)/shard_map/all_to_all | solution.py:14
  73.9 198.6 %all-gather.2.cloned.1.call-start = ((), (), s32[]{:S(2)}) async-start(), calls=%async_computation.2 | async-start | bytes 1064960 | tf_op jit(solution)/shard_map/all_gather | solution.py:72
Sparse Core Ops, SparseCore 0:
  142.9 129.5 all-gather.1
